TPU v7x, 128 devices: a whole 4x4x4 slice. The times are simulated.
128 devices in a mesh: tm: 32 (over x, z, core), feat: 4 (over y).
Axes of the slice: x: 4, y: 4, z: 4, core: 2. Of those that a mesh axis runs over, the one named last changes fastest.
Arguments:
- activations: bfloat16 [81920, 2048], P(('tm', 'feat')), may hold values from -19 to 19
- targets: bfloat16 [81920, 128], P(('tm', 'feat')), may hold values from -8 to 8
- span_of: int32 [81920], P(('tm', 'feat')), may hold values from 0 to 31, as said below
Outputs:
- predictions: bfloat16 [81920, 128], P(('tm', 'feat'))
- surprise: float32 [81920], P(('tm', 'feat'))
Inputs may be any that keep to these rules, and one draw needn't show every extreme that they name: `span_of`: in each aligned block of 640 rows (the rows of one device) every span from 0 to 31 appears exactly 20 times.
All inputs are finite; a program needn't handle non-finite values.
Results may differ from a plain program's by a relative error of at most 0.0049.
Values may be sent and summed in bfloat16 or wider, within the bound.
No kernel may reach another device: no remote copies, remote signals or barrier semaphores. Data moves between devices by JAX's collectives and lax.ppermute only.
A program may use at most 320 MiB of HBM per device.

v0:
```python
import jax
import jax.numpy as jnp
from jax import lax
from jax.sharding import Mesh, PartitionSpec as P

ITERS = 3
RIDGE = 0.1
TINY = 1e-06
TM = ("x", "z", "c")
SWAP = [(0, 1), (1, 0)]


def masked_sum(stack, position):
    keep = jnp.arange(stack.shape[0]) < position
    return jnp.sum(jnp.where(keep.reshape((-1,) + (1,) * (stack.ndim - 1)), stack, 0.0), axis=0)


def gather_feat(piece):
    n = lax.axis_size("feat")
    parts = [piece] + [
        lax.ppermute(piece, "feat", [(i, (i - k) % n) for i in range(n)]) for k in range(1, n)
    ]
    return jnp.concatenate(parts, axis=0)


def rotate(a, start, size, axis):
    return lax.dynamic_slice_in_dim(jnp.concatenate([a, a], axis=axis), start, size, axis)


def exclusive_prefix(block):
    ci = lax.axis_index("c")
    zi = lax.axis_index("z")
    xi = lax.axis_index("x")
    rows = block.shape[0]
    half = rows // 2
    partner = lax.ppermute(block, "c", SWAP)
    chip = block + partner
    below = jnp.where(ci == 1, partner, 0.0)
    mine = lax.dynamic_slice_in_dim(chip, ci * half, half, 0)
    along_z = lax.all_gather(mine, "z")
    before_z = masked_sum(along_z, zi)
    total_z = jnp.sum(along_z, axis=0)
    quarter = half // lax.axis_size("z")
    piece = lax.dynamic_slice_in_dim(total_z, zi * quarter, quarter, 0)
    along_x = lax.all_gather(piece, "x")
    before_x = lax.all_gather(masked_sum(along_x, xi), "z", axis=0, tiled=True)
    mine_prefix = before_x + before_z
    other_prefix = lax.ppermute(mine_prefix, "c", SWAP)
    first = ci == 0
    top = jnp.where(first, mine_prefix, other_prefix)
    bottom = jnp.where(first, other_prefix, mine_prefix)
    return jnp.concatenate([top, bottom], axis=0) + below


def body(activations, targets, span_of):
    spans = lax.axis_size(TM)
    feat_count = lax.axis_size("feat")
    tok_dev, width = activations.shape
    n_targets = targets.shape[1]
    block_rows = width // feat_count
    share = tok_dev // spans
    contract = (((0,), (0,)), ((), ()))
    highest = lax.Precision.HIGHEST
    hot = (span_of[:, None] == jnp.arange(spans)[None, :]).astype(jnp.float32)
    earlier = (jnp.arange(tok_dev)[:, None] > jnp.arange(tok_dev)[None, :]).astype(jnp.float32)
    before = jnp.dot(earlier, hot, precision=highest, preferred_element_type=jnp.float32)
    rank = jnp.sum(before * hot, axis=1).astype(jnp.int32)
    dest = span_of * share + rank
    permute = (dest[None, :] == jnp.arange(tok_dev)[:, None]).astype(jnp.bfloat16)
    joined_in = jnp.concatenate([activations, targets], axis=1)
    sorted_xy = jnp.dot(permute, joined_in, preferred_element_type=jnp.float32).astype(jnp.bfloat16)
    sorted_xy = sorted_xy.reshape(spans, share, width + n_targets)
    moved = lax.all_to_all(sorted_xy, TM, split_axis=0, concat_axis=0, tiled=True)
    local_xy = moved.reshape(tok_dev, width + n_targets)
    local_x = local_xy[:, :width]
    col_start = lax.axis_index("feat") * block_rows
    rows_xy = lax.all_gather(local_xy, "feat", axis=0, tiled=True)
    own = lax.dynamic_slice_in_dim(rows_xy, col_start, block_rows, 1)
    moments = exclusive_prefix(
        lax.dot_general(own, rows_xy, contract, preferred_element_type=jnp.float32)
    )
    fi = lax.axis_index("feat")
    gram_prefix = rotate(moments[:, :width], fi * block_rows, width, 1)
    cross_prefix = gather_feat(moments[:, width:])
    span = (lax.axis_index("x") * lax.axis_size("z") + lax.axis_index("z")) * lax.axis_size(
        "c"
    ) + lax.axis_index("c")
    seen = (span * (tok_dev * feat_count)).astype(jnp.float32)
    scale = 1.0 / jnp.maximum(seen, 1.0)
    rhs = scale * cross_prefix
    residual = rhs
    direction = rhs
    norm_now = jnp.sum(residual * residual, axis=0)
    solution = None
    for step in range(ITERS):
        product = jnp.dot(
            gram_prefix, direction, precision=lax.Precision.HIGH, preferred_element_type=jnp.float32
        )
        own_image = scale * product + RIDGE * direction[:block_rows]
        if step + 1 < ITERS:
            image = gather_feat(own_image)
            curvature = jnp.sum(direction * image, axis=0)
        else:
            partial = jnp.sum(direction[:block_rows] * own_image, axis=0, keepdims=True)
            curvature = jnp.sum(gather_feat(partial), axis=0)
        alpha = norm_now / (curvature + TINY)
        update = alpha * direction
        solution = update if solution is None else solution + update
        if step + 1 < ITERS:
            residual = residual - alpha * image
            norm_next = jnp.sum(residual * residual, axis=0)
            direction = residual + norm_next / (norm_now + TINY) * direction
            norm_now = norm_next
    weights = rotate(
        solution.astype(jnp.bfloat16), (feat_count - fi) % feat_count * block_rows, width, 0
    )
    predicted = jnp.dot(local_x, weights, preferred_element_type=jnp.float32).astype(jnp.bfloat16)
    returned = lax.all_to_all(
        predicted.reshape(spans, share, n_targets), TM, split_axis=0, concat_axis=0, tiled=True
    )
    in_order = returned.reshape(tok_dev, n_targets)
    predictions = lax.dot_general(
        permute, in_order, (((0,), (0,)), ((), ())), preferred_element_type=jnp.float32
    ).astype(jnp.bfloat16)
    error = targets.astype(jnp.float32) - predictions.astype(jnp.float32)
    surprise = jnp.mean(error * error, axis=1)
    return (predictions, surprise)


def solution(mesh):
    tm = mesh.shape["tm"]
    feat = mesh.shape["feat"]
    fine = Mesh(mesh.devices.reshape(tm // 8, 4, 2, feat), TM + ("feat",))
    rows = TM + ("feat",)
    return jax.shard_map(
        body,
        mesh=fine,
        in_specs=(P(rows, None), P(rows, None), P(rows)),
        out_specs=(P(rows, None), P(rows)),
        check_vma=False,
    )
```

profile of v0, /device:TPU:1, one launch (start us, length us, event | category | flops | bytes accessed | tf_op | source)
XLA Modules:
  0.0 470.7 jit_solution(7356976778085991904)
XLA Ops:
  7.2 1.1 fusion.20
  8.3 0.7 convert_add_fusion
  9.0 5.8 %convolution_convert_fusion = bf16[640,2176]{1,0:T(8,128)(2,1)} fusion(bf16[640,128]{1,0:T(8,128)(2,1)} %param.4, bf16[640,2048]{1,0:T(8,128)(2,1)} %param.3, s32[640]{0:T(1024)S(1)} %convert_add_fusion), kind=kOutput, calls=%fused_computation.3 | convolution fusion | flops 1789952000 | bytes 5573120 | tf_op jit(solution)/shard_map/dot_general | solution.py:71
  14.8 3.6 reshape.65
  18.3 51.3 %all_to_all.10 = bf16[32,20,2176]{2,1,0:T(8,128)(2,1)} all-to-all(bf16[32,20,2176]{2,1,0:T(8,128)(2,1)S(1)} %reshape.65), channel_id=1, replica_groups=mesh['x'=4,'z'=4,'c'=2,'feat'=4] {'x','z','c'}, dimensions={0} | all-to-all | bytes 5570560 | tf_op jit(solution)/shard_map/all_to_all | solution.py:73
  69.7 5.3 %reshape.66 = bf16[640,2176]{1,0:T(8,128)(2,1)} reshape(bf16[32,20,2176]{2,1,0:T(8,128)(2,1)} %all_to_all.10) | data formatting | bytes 5570560 | tf_op jit(solution)/shard_map/reshape | solution.py:74
  75.0 103.8 %all-gather.7.cloned.1.call-done = bf16[2560,2176]{1,0:T(8,128)(2,1)} async-done(((bf16[640,2176]{1,0:T(8,128)(2,1)}), bf16[2560,2176]{1,0:T(8,128)(2,1)}) %all-gather.7.cloned.1.call-update) | async-done | bytes 11141136 | tf_op jit(solution)/shard_map/all_gather | solution.py:77
  178.8 12.5 %fusion.6 = f32[512,2176]{1,0:T(8,128)} fusion(bf16[2560,2176]{1,0:T(8,128)(2,1)} %all-gather.7.cloned.1.call-done, s32[]{:T(128)S(6)} %select_n.51), kind=kOutput, calls=%fused_computation.11 | convolution fusion | flops 5704253440 | bytes 18219012 | tf_op jit(solution)/shard_map/dot_general | solution.py:80
  191.2 0.8 collective-permute-start
  192.1 7.5 %collective-permute-done = f32[512,2176]{1,0:T(8,128)} collective-permute-done((f32[512,2176]{1,0:T(8,128)}, f32[512,2176]{1,0:T(8,128)}, u32[]{:S(2)}, u32[]{:S(2)}) %collective-permute-start) | collective-permute-done | bytes 4456480 | tf_op jit(solution)/shard_map/ppermute | solution.py:36
  199.6 3.9 dynamic-slice_add_fusion
  203.6 88.2 %all-gather.11.cloned.1.call-done = f32[1024,2176]{1,0:T(8,128)} async-done(((f32[256,2176]{1,0:T(8,128)}), f32[1024,2176]{1,0:T(8,128)}) %all-gather.11.cloned.1.call-update) | async-done | bytes 8912912 | tf_op jit(solution)/shard_map/all_gather | solution.py:40
  291.8 5.1 %select_reduce_fusion = (f32[256,2176]{1,0:T(8,128)S(1)}, f32[256,2176]{1,0:T(8,128)S(1)}) fusion(f32[4,256,2176]{2,1,0:T(8,128)} %bitcast.18, pred[4]{0:T(512)(128)(4,1)S(1)} %iota_compare_fusion.13), kind=kLoop, calls=%fused_computation | loop fusion | flops 5570560 | bytes 13369348 | tf_op jit(solution)/shard_map/reduce_sum | solution.py:15
  296.9 0.8 constant_dynamic-slice_fusion
  297.9 32.8 %all-gather.13.cloned.1.call-done = f32[256,2176]{1,0:T(8,128)} async-done(((f32[64,2176]{1,0:T(8,128)}), f32[256,2176]{1,0:T(8,128)}) %all-gather.13.cloned.1.call-update) | async-done | bytes 2228240 | tf_op jit(solution)/shard_map/all_gather | solution.py:45
  330.6 2.7 select_reduce_fusion.1
  333.4 32.3 %all-gather.9.cloned.1.call-done = f32[256,2176]{1,0:T(8,128)} async-done(((f32[64,2176]{1,0:T(8,128)}), f32[256,2176]{1,0:T(8,128)}) %all-gather.9.cloned.1.call-update) | async-done | bytes 2228240 | tf_op jit(solution)/shard_map/all_gather | solution.py:46
  365.7 3.2 add.97
  368.9 0.8 collective-permute-start.1
  369.7 4.1 collective-permute-done.1
  373.9 1.9 broadcast_select_fusion.1
  375.8 2.7 maximum_add_fusion
  378.5 0.5 slice.27
  379.1 2.5 collective-permute-start.2
  381.6 0.5 collective-permute-start.3
  382.2 0.6 collective-permute-start.4
  382.8 1.0 fusion
  383.8 8.2 %collective-permute-done.2 = f32[512,128]{1,0:T(8,128)S(1)} collective-permute-done((f32[512,128]{1,0:T(8,128)S(1)}, f32[512,128]{1,0:T(8,128)S(1)}, u32[]{:S(2)}, u32[]{:S(2)}) %collective-permute-start.2) | collective-permute-done | bytes 262176 | tf_op jit(solution)/shard_map/ppermute | solution.py:21
  392.0 3.9 collective-permute-done.4
  395.9 0.1 maximum_multiply_fusion
  395.9 1.8 fusion.13
  397.7 0.2 collective-permute-start.5
  397.9 0.5 collective-permute-start.6
  398.5 0.8 collective-permute-start.7
  399.3 6.0 %collective-permute-done.5 = f32[512,128]{1,0:T(8,128)S(1)} collective-permute-done((f32[512,128]{1,0:T(8,128)S(1)}, f32[512,128]{1,0:T(8,128)S(1)}, u32[]{:S(2)}, u32[]{:S(2)}) %collective-permute-start.5) | collective-permute-done | bytes 262176 | tf_op jit(solution)/shard_map/ppermute | solution.py:21
  405.3 1.7 collective-permute-done.6
  407.0 6.3 %collective-permute-done.7 = f32[512,128]{1,0:T(8,128)S(1)} collective-permute-done((f32[512,128]{1,0:T(8,128)S(1)}, f32[512,128]{1,0:T(8,128)S(1)}, u32[]{:S(2)}, u32[]{:S(2)}) %collective-permute-start.7) | collective-permute-done | bytes 262176 | tf_op jit(solution)/shard_map/ppermute | solution.py:21
  413.3 0.3 multiply_reduce_fusion.3
  413.6 0.3 multiply_reduce_fusion.2
  414.0 0.2 multiply_add_fusion.1
  414.2 1.8 fusion.12
  416.0 0.1 collective-permute-start.10
  416.1 2.7 collective-permute-start.8
  418.7 11.5 %collective-permute-done.10 = f32[512,128]{1,0:T(8,128)S(1)} collective-permute-done((f32[512,128]{1,0:T(8,128)S(1)}, f32[512,128]{1,0:T(8,128)S(1)}, u32[]{:S(2)}, u32[]{:S(2)}) %collective-permute-start.10) | collective-permute-done | bytes 262176 | tf_op jit(solution)/shard_map/ppermute | solution.py:21
  430.3 0.3 multiply_reduce_fusion.1
  430.6 0.4 copy-done.7
  431.0 0.1 copy-done.8
  431.1 0.1 copy-done.9
  431.2 1.9 multiply_reduce_fusion
  433.0 0.1 multiply_add_fusion
  433.1 0.7 copy-done.1
  433.9 1.9 fusion.18
  435.8 2.4 collective-permute-start.11
  438.1 0.7 collective-permute-start.13
  438.9 3.2 collective-permute-done.12
  442.1 0.3 add_convert_fusion
  442.4 2.2 fusion.14
  444.6 0.7 reshape.67
  445.3 8.7 %all-to-all-start.1 = ((bf16[32,20,128]{2,1,0:T(8,128)(2,1)}), bf16[32,20,128]{2,1,0:T(8,128)(2,1)S(1)}, u32[]{:S(2)}, u32[]{:S(2)}) async-start(bf16[32,20,128]{2,1,0:T(8,128)(2,1)} %reshape.67), calls=%async_computation.1 | async-start | bytes 393216 | tf_op jit(solution)/shard_map/all_to_all | solution.py:118
  454.0 0.2 copy.9
  454.1 8.1 %all-to-all-done.1 = bf16[32,20,128]{2,1,0:T(8,128)(2,1)S(1)} async-done(((bf16[32,20,128]{2,1,0:T(8,128)(2,1)}), bf16[32,20,128]{2,1,0:T(8,128)(2,1)S(1)}, u32[]{:S(2)}, u32[]{:S(2)}) %all-to-all-start.1) | async-done | bytes 163872 | tf_op jit(solution)/shard_map/all_to_all | solution.py:118
  462.3 0.5 multiply_reduce_fusion.5
  462.8 0.8 copy.10
  463.6 0.6 broadcast_multiply_fusion
  (42 shorter events, 0.4 us)
Async XLA Ops:
  7.2 171.6 %all-gather.7.cloned.1.call-start = ((), (), s32[]{:S(2)}) async-start(), calls=%async_computation.2 | async-start | bytes 13926400 | tf_op jit(solution)/shard_map/all_gather | solution.py:77
  74.9 216.8 %all-gather.11.cloned.1.call-start = ((), (), s32[]{:S(2)}) async-start(), calls=%async_computation.4 | async-start | bytes 11141120 | tf_op jit(solution)/shard_map/all_gather | solution.py:40
  191.2 8.3 %collective-permute-start = (f32[512,2176]{1,0:T(8,128)}, f32[512,2176]{1,0:T(8,128)}, u32[]{:S(2)}, u32[]{:S(2)}) collective-permute-start(f32[512,2176]{1,0:T(8,128)} %fusion.6), channel_id=1, source_target_pairs={{0,4},{4,0},{1,5},{5,1},{2,6},{6,2},{3,7},{7,3},{8,12},{12,8},{9,1... | collective-permute-start | bytes 13369352 | tf_op jit(solution)/shard_map/ppermute | solution.py:36
  203.5 127.1 %all-gather.13.cloned.1.call-start = ((), (), s32[]{:S(2)}) async-start(), calls=%async_computation.5 | async-start | bytes 2785280 | tf_op jit(solution)/shard_map/all_gather | solution.py:45
  297.8 67.9 %all-gather.9.cloned.1.call-start = ((), (), s32[]{:S(2)}) async-start(), calls=%async_computation.3 | async-start | bytes 2785280 | tf_op jit(solution)/shard_map/all_gather | solution.py:46
  368.9 5.0 %collective-permute-start.1 = (f32[256,2176]{1,0:T(8,128)}, f32[256,2176]{1,0:T(8,128)S(1)}, u32[]{:S(2)}, u32[]{:S(2)}) collective-permute-start(f32[256,2176]{1,0:T(8,128)} %add.97), channel_id=1, source_target_pairs={{0,4},{4,0},{1,5},{5,1},{2,6},{6,2},{3,7},{7,3},{8,12},{12,8},{9,1... | collective-permute-start | bytes 6684680 | tf_op jit(solution)/shard_map/ppermute | solution.py:48
  379.1 12.9 %collective-permute-start.2 = (f32[512,128]{1,0:T(8,128)S(1)}, f32[512,128]{1,0:T(8,128)S(1)}, u32[]{:S(2)}, u32[]{:S(2)}) collective-permute-start(f32[512,128]{1,0:T(8,128)S(1)} %slice.26), channel_id=1, source_target_pairs={{0,3},{1,0},{2,1},{3,2},{4,7},{5,4},{6,5},{7,6},{8,11},{9,8},{10,9... | collective-permute-start | bytes 786440 | tf_op jit(solution)/shard_map/ppermute | solution.py:21
  381.6 10.3 %collective-permute-start.3 = (f32[512,128]{1,0:T(8,128)S(1)}, f32[512,128]{1,0:T(8,128)S(1)}, u32[]{:S(2)}, u32[]{:S(2)}) collective-permute-start(f32[512,128]{1,0:T(8,128)S(1)} %slice.26), channel_id=1, source_target_pairs={{0,2},{1,3},{2,0},{3,1},{4,6},{5,7},{6,4},{7,5},{8,10},{9,11},{10,... | collective-permute-start | bytes 786440 | tf_op jit(solution)/shard_map/ppermute | solution.py:21
  382.2 13.7 %collective-permute-start.4 = (f32[512,128]{1,0:T(8,128)S(1)}, f32[512,128]{1,0:T(8,128)S(1)}, u32[]{:S(2)}, u32[]{:S(2)}) collective-permute-start(f32[512,128]{1,0:T(8,128)S(1)} %slice.26), channel_id=1, source_target_pairs={{0,1},{1,2},{2,3},{3,0},{4,5},{5,6},{6,7},{7,4},{8,9},{9,10},{10,1... | collective-permute-start | bytes 786440 | tf_op jit(solution)/shard_map/ppermute | solution.py:21
  383.8 30.4 %copy-start = (f32[512,2048]{1,0:T(8,128)}, f32[512,2048]{1,0:T(8,128)S(1)}, u32[]{:S(2)}) copy-start(f32[512,2048]{1,0:T(8,128)S(1)} %fusion) | copy-start | bytes 12582916
  397.7 7.5 %collective-permute-start.5 = (f32[512,128]{1,0:T(8,128)S(1)}, f32[512,128]{1,0:T(8,128)S(1)}, u32[]{:S(2)}, u32[]{:S(2)}) collective-permute-start(f32[512,128]{1,0:T(8,128)S(1)} %fusion.13), channel_id=1, source_target_pairs={{0,3},{1,0},{2,1},{3,2},{4,7},{5,4},{6,5},{7,6},{8,11},{9,8},{10,9... | collective-permute-start | bytes 786440 | tf_op jit(solution)/shard_map/ppermute | solution.py:21
  397.9 9.0 %collective-permute-start.6 = (f32[512,128]{1,0:T(8,128)S(1)}, f32[512,128]{1,0:T(8,128)S(1)}, u32[]{:S(2)}, u32[]{:S(2)}) collective-permute-start(f32[512,128]{1,0:T(8,128)S(1)} %fusion.13), channel_id=1, source_target_pairs={{0,2},{1,3},{2,0},{3,1},{4,6},{5,7},{6,4},{7,5},{8,10},{9,11},{10,... | collective-permute-start | bytes 786440 | tf_op jit(solution)/shard_map/ppermute | solution.py:21
  398.5 14.8 %collective-permute-start.7 = (f32[512,128]{1,0:T(8,128)S(1)}, f32[512,128]{1,0:T(8,128)S(1)}, u32[]{:S(2)}, u32[]{:S(2)}) collective-permute-start(f32[512,128]{1,0:T(8,128)S(1)} %fusion.13), channel_id=1, source_target_pairs={{0,1},{1,2},{2,3},{3,0},{4,5},{5,6},{6,7},{7,4},{8,9},{9,10},{10,1... | collective-permute-start | bytes 786440 | tf_op jit(solution)/shard_map/ppermute | solution.py:21
  405.3 8.7 %copy-start.3 = (f32[512,128]{1,0:T(8,128)}, f32[512,128]{1,0:T(8,128)S(1)}, u32[]{:S(2)}) copy-start(f32[512,128]{1,0:T(8,128)S(1)} %collective-permute-done.5) | copy-start | bytes 786436
  407.0 7.0 %copy-start.4 = (f32[512,128]{1,0:T(8,128)}, f32[512,128]{1,0:T(8,128)S(1)}, u32[]{:S(2)}) copy-start(f32[512,128]{1,0:T(8,128)S(1)} %collective-permute-done.6) | copy-start | bytes 786436
  413.3 0.7 copy-start.5
  416.0 14.6 %copy-start.6 = (f32[512,128]{1,0:T(8,128)}, f32[512,128]{1,0:T(8,128)S(1)}, u32[]{:S(2)}) copy-start(f32[512,128]{1,0:T(8,128)S(1)} %fusion.12) | copy-start | bytes 786436
  416.0 14.3 %collective-permute-start.10 = (f32[512,128]{1,0:T(8,128)S(1)}, f32[512,128]{1,0:T(8,128)S(1)}, u32[]{:S(2)}, u32[]{:S(2)}) collective-permute-start(f32[512,128]{1,0:T(8,128)S(1)} %fusion.12), channel_id=1, source_target_pairs={{0,1},{1,2},{2,3},{3,0},{4,5},{5,6},{6,7},{7,4},{8,9},{9,10},{10,1... | collective-permute-start | bytes 786440 | tf_op jit(solution)/shard_map/ppermute | solution.py:21
  416.1 14.2 %collective-permute-start.8 = (f32[512,128]{1,0:T(8,128)S(1)}, f32[512,128]{1,0:T(8,128)S(1)}, u32[]{:S(2)}, u32[]{:S(2)}) collective-permute-start(f32[512,128]{1,0:T(8,128)S(1)} %fusion.12), channel_id=1, source_target_pairs={{0,3},{1,0},{2,1},{3,2},{4,7},{5,4},{6,5},{7,6},{8,11},{9,8},{10,9... | collective-permute-start | bytes 786440 | tf_op jit(solution)/shard_map/ppermute | solution.py:21
  418.7 11.5 %collective-permute-start.9 = (f32[512,128]{1,0:T(8,128)S(1)}, f32[512,128]{1,0:T(8,128)S(1)}, u32[]{:S(2)}, u32[]{:S(2)}) collective-permute-start(f32[512,128]{1,0:T(8,128)S(1)} %fusion.12), channel_id=1, source_target_pairs={{0,2},{1,3},{2,0},{3,1},{4,6},{5,7},{6,4},{7,5},{8,10},{9,11},{10,... | collective-permute-start | bytes 786440 | tf_op jit(solution)/shard_map/ppermute | solution.py:21
  430.3 0.7 copy-start.7
  430.3 0.8 copy-start.8
  430.3 0.9 copy-start.9
  431.1 2.7 copy-start.1
  435.8 3.1 collective-permute-start.11
  438.1 3.9 collective-permute-start.12
  438.1 3.9 collective-permute-start.13
  438.8 3.6 copy-start.2
  442.4 11.6 %copy-start.10 = (bf16[640,128]{1,0:T(8,128)(2,1)S(1)}, bf16[640,128]{1,0:T(8,128)(2,1)}, u32[]{:S(2)}) copy-start(bf16[640,128]{1,0:T(8,128)(2,1)} %param.4) | copy-start | bytes 491524
  445.3 17.0 %all-to-all-start.1 = ((bf16[32,20,128]{2,1,0:T(8,128)(2,1)}), bf16[32,20,128]{2,1,0:T(8,128)(2,1)S(1)}, u32[]{:S(2)}, u32[]{:S(2)}) async-start(bf16[32,20,128]{2,1,0:T(8,128)(2,1)} %reshape.67), calls=%async_computation.1 | async-start | bytes 393216 | tf_op jit(solution)/shard_map/all_to_all | solution.py:118
Sparse Core Ops, SparseCore 0:
  75.1 103.6 all-gather.6
  203.6 88.1 all-gather.10
  297.9 32.6 all-gather.12
  333.5 32.1 all-gather.8
where the time goes:
time: 471 us
  waiting for transfers between devices  318 us (68%)
  blocking collectives  51.3 us (11%)
  matrix products  27.4 us (6%)
  other arithmetic  25.3 us (5%)
  starting transfers between devices  21.5 us (5%)
  between operations  14 us (3%)
  local copies, waits for them, and re-layouts  13.3 us (3%)
    all_gather x1, waiting for transfers between devices, body(): rows_xy = lax.all_gather(local_xy, 'feat', axis=0, tiled=True)  104 us
    all_gather x1, waiting for transfers between devices, exclusive_prefix(): along_z = lax.all_gather(mine, 'z')  88.2 us
    all_to_all x1, blocking collectives, body(): lax.all_to_all(sorted_xy, TM, split_axis=0, concat_axis=0, tiled=True)  51.3 us
    ppermute x12, waiting for transfers between devices, gather_feat(): lax.ppermute(piece, 'feat', [(i, (i - k) % n) for i in range(n)])  40.9 us
    all_gather x1, waiting for transfers between devices, exclusive_prefix(): along_x = lax.all_gather(piece, 'x')  32.8 us
    all_gather x1, waiting for transfers between devices, exclusive_prefix(): before_x = lax.all_gather(masked_sum(along_x, xi), 'z', axis=0, tiled=True)  32.3 us
    dot_general x1, matrix products, body(): lax.dot_general(own, rows_xy, contract, preferred_element_type=jnp.float32)  12.5 us
    ppermute x12, starting transfers between devices, gather_feat(): lax.ppermute(piece, 'feat', [(i, (i - k) % n) for i in range(n)])  11 us
  transfers between devices with their start and end apart: 19, of which 14 were waited for; matrix products, arithmetic and copies ran while one was open for 0% of the time, Pallas kernels for 0%

commit v1 on v0

--- a/solution.py
+++ b/solution.py
@@ -2,12 +2,39 @@
 import jax.numpy as jnp
 from jax import lax
 from jax.sharding import Mesh, PartitionSpec as P
+from jax.lax import axis_index, axis_size, ppermute
 
 ITERS = 3
 RIDGE = 0.1
 TINY = 1e-06
 TM = ("x", "z", "c")
 SWAP = [(0, 1), (1, 0)]
+
+
+def _plan_view(in_array, on_dim):
+    low = axis_size("feat")
+    reached = axis_index("feat")
+    wide_out, b_next, carry = (low, reached, in_array.shape[on_dim])
+    column = [nth * wide_out if num == on_dim else nth for num, nth in enumerate(in_array.shape)]
+    r_now = jnp.zeros(column, in_array.dtype)
+    clean = lax.dynamic_update_slice_in_dim(r_now, in_array, b_next * carry, axis=on_dim)
+    block_out = all_values = in_array
+    for dd in range(1, wide_out // 2 + 1):
+        spare = map(lambda num: (num, (num + 1) % wide_out), range(wide_out))
+        taken_in = list(spare)
+        block_out = ppermute(block_out, axis_name="feat", perm=taken_in)
+        clean = lax.dynamic_update_slice_in_dim(
+            clean, block_out, (b_next - dd) % wide_out * carry, axis=on_dim
+        )
+        if 2 * dd < wide_out:
+            w_next = range(wide_out)
+            all_values = ppermute(
+                all_values, "feat", list(map(lambda num: (num, (num - 1) % wide_out), w_next))
+            )
+            clean = lax.dynamic_update_slice_in_dim(
+                clean, all_values, (b_next + dd) % wide_out * carry, axis=on_dim
+            )
+    return clean
 
 
 def masked_sum(stack, position):
@@ -74,7 +101,7 @@
     local_xy = moved.reshape(tok_dev, width + n_targets)
     local_x = local_xy[:, :width]
     col_start = lax.axis_index("feat") * block_rows
-    rows_xy = lax.all_gather(local_xy, "feat", axis=0, tiled=True)
+    rows_xy = _plan_view(local_xy, 0)
     own = lax.dynamic_slice_in_dim(rows_xy, col_start, block_rows, 1)
     moments = exclusive_prefix(
         lax.dot_general(own, rows_xy, contract, preferred_element_type=jnp.float32)

time: 471 us -> 488 us (1.036)
  local copies, waits for them, and re-layouts: 13.3 us -> 22.9 us
  waiting for transfers between devices: 318 us -> 324 us
    ppermute x0 -> x3, waiting for transfers between devices: none -> 116 us  [the longest x2 116 us: _plan_view(): block_out = ppermute(block_out, axis_name='feat', perm=taken_in)]
    all_gather x1 -> x0, waiting for transfers between devices: 104 us -> none  [body(): rows_xy = lax.all_gather(local_xy, 'feat', axis=0, tiled=True)]
    dynamic_update_slice x0 -> x4, local copies, waits for them, and re-layouts: none -> 8.73 us  [the longest x2 4.36 us: _plan_view(): lax.dynamic_update_slice_in_dim(clean, block_out, (b_next - dd) % wide_ou...]
    all_gather x1, waiting for transfers between devices: 88.2 us -> 82.3 us  [exclusive_prefix(): along_z = lax.all_gather(mine, 'z')]
  transfers between devices with their start and end apart: 19 -> 21, of which waited for: 14 -> 17; matrix products, arithmetic and copies ran while one was open for 0% -> 2% of each run, Pallas kernels for 0% -> 0%
where the time goes in v1:
time: 488 us; the launch traced here: 487 us
  waiting for transfers between devices  324 us (66%)
  blocking collectives  51.3 us (11%)
  other arithmetic  25.3 us (5%)
  matrix products  24.7 us (5%)
  starting transfers between devices  24.6 us (5%)
  local copies, waits for them, and re-layouts  22.9 us (5%)
  between operations  14 us (3%)
    ppermute x2, waiting for transfers between devices, _plan_view(): block_out = ppermute(block_out, axis_name='feat', perm=taken_in)  116 us
    all_gather x1, waiting for transfers between devices, exclusive_prefix(): along_z = lax.all_gather(mine, 'z')  82.3 us
    all_to_all x1, blocking collectives, body(): lax.all_to_all(sorted_xy, TM, split_axis=0, concat_axis=0, tiled=True)  51.3 us
    ppermute x12, waiting for transfers between devices, gather_feat(): lax.ppermute(piece, 'feat', [(i, (i - k) % n) for i in range(n)])  41.1 us
    all_gather x1, waiting for transfers between devices, exclusive_prefix(): along_x = lax.all_gather(piece, 'x')  32.8 us
    all_gather x1, waiting for transfers between devices, exclusive_prefix(): before_x = lax.all_gather(masked_sum(along_x, xi), 'z', axis=0, tiled=True)  32.3 us
    ppermute x12, starting transfers between devices, gather_feat(): lax.ppermute(piece, 'feat', [(i, (i - k) % n) for i in range(n)])  11 us
  transfers between devices with their start and end apart: 21, of which 17 were waited for; matrix products, arithmetic and copies ran while one was open for 2% of the time, Pallas kernels for 0%

profile of v1, /device:TPU:1, one launch (start us, length us, event | category | flops | bytes accessed | tf_op | source)
XLA Modules:
  0.0 486.7 jit_solution(2303873230479915043)
XLA Ops:
  7.2 1.1 fusion.20
  8.3 0.7 convert_add_fusion
  9.0 5.8 %convolution_convert_fusion = bf16[640,2176]{1,0:T(8,128)(2,1)} fusion(bf16[640,128]{1,0:T(8,128)(2,1)} %param.4, bf16[640,2048]{1,0:T(8,128)(2,1)} %param.3, s32[640]{0:T(1024)S(1)} %convert_add_fusion), kind=kOutput, calls=%fused_computation.3 | convolution fusion | flops 1789952000 | bytes 5573120 | tf_op jit(solution)/shard_map/dot_general | solution.py:98
  14.7 3.6 reshape.65
  18.3 51.3 %all_to_all.10 = bf16[32,20,2176]{2,1,0:T(8,128)(2,1)} all-to-all(bf16[32,20,2176]{2,1,0:T(8,128)(2,1)S(1)} %reshape.65), channel_id=1, replica_groups=mesh['x'=4,'z'=4,'c'=2,'feat'=4] {'x','z','c'}, dimensions={0} | all-to-all | bytes 5570560 | tf_op jit(solution)/shard_map/all_to_all | solution.py:100
  69.7 5.3 %reshape.66 = bf16[640,2176]{1,0:T(8,128)(2,1)} reshape(bf16[32,20,2176]{2,1,0:T(8,128)(2,1)} %all_to_all.10) | data formatting | bytes 5570560 | tf_op jit(solution)/shard_map/reshape | solution.py:101
  74.9 1.3 collective-permute-start
  76.2 1.4 collective-permute-start.1
  77.7 60.5 %collective-permute-done = bf16[640,2176]{1,0:T(8,128)(2,1)} collective-permute-done((bf16[640,2176]{1,0:T(8,128)(2,1)}, bf16[640,2176]{1,0:T(8,128)(2,1)}, u32[]{:S(2)}, u32[]{:S(2)}) %collective-permute-start) | collective-permute-done | bytes 2785312 | tf_op jit(solution)/shard_map/ppermute | solution.py:25
  138.2 0.8 broadcast_in_dim.48
  139.0 2.2 constant_dynamic-update-slice_fusion.3
  141.2 2.2 constant_dynamic-update-slice_fusion.2
  143.4 2.2 constant_dynamic-update-slice_fusion.1
  145.6 55.0 %collective-permute-done.2 = bf16[640,2176]{1,0:T(8,128)(2,1)} collective-permute-done((bf16[640,2176]{1,0:T(8,128)(2,1)}, bf16[640,2176]{1,0:T(8,128)(2,1)}, u32[]{:S(2)}, u32[]{:S(2)}) %collective-permute-start.2) | collective-permute-done | bytes 2785312 | tf_op jit(solution)/shard_map/ppermute | solution.py:25
  200.6 2.2 constant_dynamic-update-slice_fusion
  202.8 8.0 %fusion.6 = f32[512,2176]{1,0:T(8,128)} fusion(bf16[2560,2176]{1,0:T(8,128)(2,1)S(1)} %constant_dynamic-update-slice_fusion, s32[]{:T(128)S(6)} %select_n.82), kind=kOutput, calls=%fused_computation.11 | convolution fusion | flops 5704253440 | bytes 18219012 | tf_op jit(solution)/shard_map/dot_general | solution.py:107
  210.7 2.0 collective-permute-start.3
  212.7 7.5 %collective-permute-done.3 = f32[512,2176]{1,0:T(8,128)} collective-permute-done((f32[512,2176]{1,0:T(8,128)}, f32[512,2176]{1,0:T(8,128)}, u32[]{:S(2)}, u32[]{:S(2)}) %collective-permute-start.3) | collective-permute-done | bytes 4456480 | tf_op jit(solution)/shard_map/ppermute | solution.py:63
  220.2 3.9 dynamic-slice_add_fusion
  224.4 82.3 %all-gather.8.cloned.1.call-done = f32[1024,2176]{1,0:T(8,128)} async-done(((f32[256,2176]{1,0:T(8,128)}), f32[1024,2176]{1,0:T(8,128)}) %all-gather.8.cloned.1.call-update) | async-done | bytes 8912912 | tf_op jit(solution)/shard_map/all_gather | solution.py:67
  306.6 5.1 %select_reduce_fusion = (f32[256,2176]{1,0:T(8,128)S(1)}, f32[256,2176]{1,0:T(8,128)S(1)}) fusion(f32[4,256,2176]{2,1,0:T(8,128)} %bitcast.18, pred[4]{0:T(512)(128)(4,1)S(1)} %iota_compare_fusion.13), kind=kLoop, calls=%fused_computation | loop fusion | flops 5570560 | bytes 13369348 | tf_op jit(solution)/shard_map/reduce_sum | solution.py:42
  311.7 0.8 constant_dynamic-slice_fusion
  312.7 32.8 %all-gather.10.cloned.1.call-done = f32[256,2176]{1,0:T(8,128)} async-done(((f32[64,2176]{1,0:T(8,128)}), f32[256,2176]{1,0:T(8,128)}) %all-gather.10.cloned.1.call-update) | async-done | bytes 2228240 | tf_op jit(solution)/shard_map/all_gather | solution.py:72
  345.5 2.7 select_reduce_fusion.1
  348.2 32.3 %all-gather.6.cloned.1.call-done = f32[256,2176]{1,0:T(8,128)} async-done(((f32[64,2176]{1,0:T(8,128)}), f32[256,2176]{1,0:T(8,128)}) %all-gather.6.cloned.1.call-update) | async-done | bytes 2228240 | tf_op jit(solution)/shard_map/all_gather | solution.py:73
  380.5 3.2 add.131
  383.7 0.8 collective-permute-start.4
  384.6 4.1 collective-permute-done.4
  388.7 1.9 broadcast_select_fusion.1
  390.6 2.7 maximum_add_fusion
  393.4 0.5 slice.27
  393.9 2.5 collective-permute-start.5
  396.5 0.5 collective-permute-start.6
  397.0 0.6 collective-permute-start.7
  397.6 1.0 fusion
  398.6 8.2 %collective-permute-done.5 = f32[512,128]{1,0:T(8,128)S(1)} collective-permute-done((f32[512,128]{1,0:T(8,128)S(1)}, f32[512,128]{1,0:T(8,128)S(1)}, u32[]{:S(2)}, u32[]{:S(2)}) %collective-permute-start.5) | collective-permute-done | bytes 262176 | tf_op jit(solution)/shard_map/ppermute | solution.py:48
  406.8 3.9 collective-permute-done.7
  410.8 1.8 fusion.13
  412.7 2.7 collective-permute-start.8
  415.3 11.6 %collective-permute-done.10 = f32[512,128]{1,0:T(8,128)S(1)} collective-permute-done((f32[512,128]{1,0:T(8,128)S(1)}, f32[512,128]{1,0:T(8,128)S(1)}, u32[]{:S(2)}, u32[]{:S(2)}) %collective-permute-start.10) | collective-permute-done | bytes 262176 | tf_op jit(solution)/shard_map/ppermute | solution.py:48
  427.0 0.3 multiply_reduce_fusion.3
  427.3 0.3 multiply_reduce_fusion.2
  428.1 1.8 fusion.12
  429.9 2.4 collective-permute-start.11
  432.2 0.7 collective-permute-start.13
  432.9 3.8 collective-permute-done.11
  436.7 3.2 collective-permute-done.12
  439.9 7.1 %collective-permute-done.13 = f32[512,128]{1,0:T(8,128)S(1)} collective-permute-done((f32[512,128]{1,0:T(8,128)S(1)}, f32[512,128]{1,0:T(8,128)S(1)}, u32[]{:S(2)}, u32[]{:S(2)}) %collective-permute-start.13) | collective-permute-done | bytes 262176 | tf_op jit(solution)/shard_map/ppermute | solution.py:48
  447.3 0.4 copy-done.8
  447.7 1.9 multiply_reduce_fusion
  449.7 0.7 copy-done.1
  450.5 1.9 fusion.18
  452.4 0.5 collective-permute-start.15
  452.9 0.9 collective-permute-start.16
  453.9 0.9 collective-permute-done.14
  454.8 1.6 collective-permute-done.15
  456.4 0.8 collective-permute-done.16
  457.5 3.9 fusion.14
  461.4 0.7 reshape.67
  462.1 7.8 %all-to-all-start.1 = ((bf16[32,20,128]{2,1,0:T(8,128)(2,1)}), bf16[32,20,128]{2,1,0:T(8,128)(2,1)S(1)}, u32[]{:S(2)}, u32[]{:S(2)}) async-start(bf16[32,20,128]{2,1,0:T(8,128)(2,1)} %reshape.67), calls=%async_computation.1 | async-start | bytes 393216 | tf_op jit(solution)/shard_map/all_to_all | solution.py:145
  470.1 8.1 %all-to-all-done.1 = bf16[32,20,128]{2,1,0:T(8,128)(2,1)S(1)} async-done(((bf16[32,20,128]{2,1,0:T(8,128)(2,1)}), bf16[32,20,128]{2,1,0:T(8,128)(2,1)S(1)}, u32[]{:S(2)}, u32[]{:S(2)}) %all-to-all-start.1) | async-done | bytes 163872 | tf_op jit(solution)/shard_map/all_to_all | solution.py:145
  478.3 0.5 multiply_reduce_fusion.5
  478.8 0.8 copy.10
  479.6 0.6 broadcast_multiply_fusion
  (48 shorter events, 2.0 us)
Async XLA Ops:
  7.2 299.5 %all-gather.8.cloned.1.call-start = ((), (), s32[]{:S(2)}) async-start(), calls=%async_computation.3 | async-start | bytes 11141120 | tf_op jit(solution)/shard_map/all_gather | solution.py:67
  74.9 63.3 %collective-permute-start = (bf16[640,2176]{1,0:T(8,128)(2,1)}, bf16[640,2176]{1,0:T(8,128)(2,1)}, u32[]{:S(2)}, u32[]{:S(2)}) collective-permute-start(bf16[640,2176]{1,0:T(8,128)(2,1)} %reshape.66), channel_id=1, source_target_pairs={{0,1},{1,2},{2,3},{3,0},{4,5},{5,6},{6,7},{7,4},{8,9},{9,10},{10,1... | collective-permute-start | bytes 8355848 | tf_op jit(solution)/shard_map/ppermute | solution.py:25
  76.2 67.1 %collective-permute-start.1 = (bf16[640,2176]{1,0:T(8,128)(2,1)}, bf16[640,2176]{1,0:T(8,128)(2,1)}, u32[]{:S(2)}, u32[]{:S(2)}) collective-permute-start(bf16[640,2176]{1,0:T(8,128)(2,1)} %reshape.66), channel_id=1, source_target_pairs={{0,3},{1,0},{2,1},{3,2},{4,7},{5,4},{6,5},{7,6},{8,11},{9,8},{10,9... | collective-permute-start | bytes 8355848 | tf_op jit(solution)/shard_map/ppermute | solution.py:31
  138.2 62.4 %collective-permute-start.2 = (bf16[640,2176]{1,0:T(8,128)(2,1)}, bf16[640,2176]{1,0:T(8,128)(2,1)}, u32[]{:S(2)}, u32[]{:S(2)}) collective-permute-start(bf16[640,2176]{1,0:T(8,128)(2,1)} %collective-permute-done), channel_id=1, source_target_pairs={{0,1},{1,2},{2,3},{3,0},{4,5},{5,6},{6,7},{7,4},{8,9},{9,10},{10,1... | collective-permute-start | bytes 8355848 | tf_op jit(solution)/shard_map/ppermute | solution.py:25
  210.7 9.5 %collective-permute-start.3 = (f32[512,2176]{1,0:T(8,128)}, f32[512,2176]{1,0:T(8,128)}, u32[]{:S(2)}, u32[]{:S(2)}) collective-permute-start(f32[512,2176]{1,0:T(8,128)} %fusion.6), channel_id=1, source_target_pairs={{0,4},{4,0},{1,5},{5,1},{2,6},{6,2},{3,7},{7,3},{8,12},{12,8},{9,1... | collective-permute-start | bytes 13369352 | tf_op jit(solution)/shard_map/ppermute | solution.py:63
  224.1 121.4 %all-gather.10.cloned.1.call-start = ((), (), s32[]{:S(2)}) async-start(), calls=%async_computation.4 | async-start | bytes 2785280 | tf_op jit(solution)/shard_map/all_gather | solution.py:72
  312.6 67.9 %all-gather.6.cloned.1.call-start = ((), (), s32[]{:S(2)}) async-start(), calls=%async_computation.2 | async-start | bytes 2785280 | tf_op jit(solution)/shard_map/all_gather | solution.py:73
  383.7 5.0 %collective-permute-start.4 = (f32[256,2176]{1,0:T(8,128)}, f32[256,2176]{1,0:T(8,128)S(1)}, u32[]{:S(2)}, u32[]{:S(2)}) collective-permute-start(f32[256,2176]{1,0:T(8,128)} %add.131), channel_id=1, source_target_pairs={{0,4},{4,0},{1,5},{5,1},{2,6},{6,2},{3,7},{7,3},{8,12},{12,8},{9,1... | collective-permute-start | bytes 6684680 | tf_op jit(solution)/shard_map/ppermute | solution.py:75
  393.9 12.9 %collective-permute-start.5 = (f32[512,128]{1,0:T(8,128)S(1)}, f32[512,128]{1,0:T(8,128)S(1)}, u32[]{:S(2)}, u32[]{:S(2)}) collective-permute-start(f32[512,128]{1,0:T(8,128)S(1)} %slice.26), channel_id=1, source_target_pairs={{0,3},{1,0},{2,1},{3,2},{4,7},{5,4},{6,5},{7,6},{8,11},{9,8},{10,9... | collective-permute-start | bytes 786440 | tf_op jit(solution)/shard_map/ppermute | solution.py:48
  396.5 10.3 %collective-permute-start.6 = (f32[512,128]{1,0:T(8,128)S(1)}, f32[512,128]{1,0:T(8,128)S(1)}, u32[]{:S(2)}, u32[]{:S(2)}) collective-permute-start(f32[512,128]{1,0:T(8,128)S(1)} %slice.26), channel_id=1, source_target_pairs={{0,2},{1,3},{2,0},{3,1},{4,6},{5,7},{6,4},{7,5},{8,10},{9,11},{10,... | collective-permute-start | bytes 786440 | tf_op jit(solution)/shard_map/ppermute | solution.py:48
  397.0 13.7 %collective-permute-start.7 = (f32[512,128]{1,0:T(8,128)S(1)}, f32[512,128]{1,0:T(8,128)S(1)}, u32[]{:S(2)}, u32[]{:S(2)}) collective-permute-start(f32[512,128]{1,0:T(8,128)S(1)} %slice.26), channel_id=1, source_target_pairs={{0,1},{1,2},{2,3},{3,0},{4,5},{5,6},{6,7},{7,4},{8,9},{9,10},{10,1... | collective-permute-start | bytes 786440 | tf_op jit(solution)/shard_map/ppermute | solution.py:48
  398.6 29.4 %copy-start = (f32[512,2048]{1,0:T(8,128)}, f32[512,2048]{1,0:T(8,128)S(1)}, u32[]{:S(2)}) copy-start(f32[512,2048]{1,0:T(8,128)S(1)} %fusion) | copy-start | bytes 12582916
  412.6 14.4 %collective-permute-start.10 = (f32[512,128]{1,0:T(8,128)S(1)}, f32[512,128]{1,0:T(8,128)S(1)}, u32[]{:S(2)}, u32[]{:S(2)}) collective-permute-start(f32[512,128]{1,0:T(8,128)S(1)} %fusion.13), channel_id=1, source_target_pairs={{0,1},{1,2},{2,3},{3,0},{4,5},{5,6},{6,7},{7,4},{8,9},{9,10},{10,1... | collective-permute-start | bytes 786440 | tf_op jit(solution)/shard_map/ppermute | solution.py:48
  412.7 14.3 %collective-permute-start.8 = (f32[512,128]{1,0:T(8,128)S(1)}, f32[512,128]{1,0:T(8,128)S(1)}, u32[]{:S(2)}, u32[]{:S(2)}) collective-permute-start(f32[512,128]{1,0:T(8,128)S(1)} %fusion.13), channel_id=1, source_target_pairs={{0,3},{1,0},{2,1},{3,2},{4,7},{5,4},{6,5},{7,6},{8,11},{9,8},{10,9... | collective-permute-start | bytes 786440 | tf_op jit(solution)/shard_map/ppermute | solution.py:48
  415.3 11.6 %collective-permute-start.9 = (f32[512,128]{1,0:T(8,128)S(1)}, f32[512,128]{1,0:T(8,128)S(1)}, u32[]{:S(2)}, u32[]{:S(2)}) collective-permute-start(f32[512,128]{1,0:T(8,128)S(1)} %fusion.13), channel_id=1, source_target_pairs={{0,2},{1,3},{2,0},{3,1},{4,6},{5,7},{6,4},{7,5},{8,10},{9,11},{10,... | collective-permute-start | bytes 786440 | tf_op jit(solution)/shard_map/ppermute | solution.py:48
  426.9 0.7 copy-start.2
  427.0 0.8 copy-start.3
  427.0 0.9 copy-start.4
  429.9 17.4 %copy-start.5 = (f32[512,128]{1,0:T(8,128)}, f32[512,128]{1,0:T(8,128)S(1)}, u32[]{:S(2)}) copy-start(f32[512,128]{1,0:T(8,128)S(1)} %fusion.12) | copy-start | bytes 786436
  429.9 6.8 %collective-permute-start.11 = (f32[512,128]{1,0:T(8,128)S(1)}, f32[512,128]{1,0:T(8,128)S(1)}, u32[]{:S(2)}, u32[]{:S(2)}) collective-permute-start(f32[512,128]{1,0:T(8,128)S(1)} %fusion.12), channel_id=1, source_target_pairs={{0,3},{1,0},{2,1},{3,2},{4,7},{5,4},{6,5},{7,6},{8,11},{9,8},{10,9... | collective-permute-start | bytes 786440 | tf_op jit(solution)/shard_map/ppermute | solution.py:48
  432.2 7.6 %collective-permute-start.12 = (f32[512,128]{1,0:T(8,128)S(1)}, f32[512,128]{1,0:T(8,128)S(1)}, u32[]{:S(2)}, u32[]{:S(2)}) collective-permute-start(f32[512,128]{1,0:T(8,128)S(1)} %fusion.12), channel_id=1, source_target_pairs={{0,2},{1,3},{2,0},{3,1},{4,6},{5,7},{6,4},{7,5},{8,10},{9,11},{10,... | collective-permute-start | bytes 786440 | tf_op jit(solution)/shard_map/ppermute | solution.py:48
  432.2 14.8 %collective-permute-start.13 = (f32[512,128]{1,0:T(8,128)S(1)}, f32[512,128]{1,0:T(8,128)S(1)}, u32[]{:S(2)}, u32[]{:S(2)}) collective-permute-start(f32[512,128]{1,0:T(8,128)S(1)} %fusion.12), channel_id=1, source_target_pairs={{0,1},{1,2},{2,3},{3,0},{4,5},{5,6},{6,7},{7,4},{8,9},{9,10},{10,1... | collective-permute-start | bytes 786440 | tf_op jit(solution)/shard_map/ppermute | solution.py:48
  436.7 10.6 %copy-start.6 = (f32[512,128]{1,0:T(8,128)}, f32[512,128]{1,0:T(8,128)S(1)}, u32[]{:S(2)}) copy-start(f32[512,128]{1,0:T(8,128)S(1)} %collective-permute-done.11) | copy-start | bytes 786436
  439.9 7.4 %copy-start.7 = (f32[512,128]{1,0:T(8,128)}, f32[512,128]{1,0:T(8,128)S(1)}, u32[]{:S(2)}) copy-start(f32[512,128]{1,0:T(8,128)S(1)} %collective-permute-done.12) | copy-start | bytes 786436
  447.0 0.7 copy-start.8
  447.7 2.7 copy-start.1
  452.3 2.5 collective-permute-start.14
  452.4 4.0 collective-permute-start.15
  452.9 4.3 collective-permute-start.16
  457.5 12.5 %copy-start.9 = (bf16[640,128]{1,0:T(8,128)(2,1)S(1)}, bf16[640,128]{1,0:T(8,128)(2,1)}, u32[]{:S(2)}) copy-start(bf16[640,128]{1,0:T(8,128)(2,1)} %param.4) | copy-start | bytes 491524
  462.1 16.1 %all-to-all-start.1 = ((bf16[32,20,128]{2,1,0:T(8,128)(2,1)}), bf16[32,20,128]{2,1,0:T(8,128)(2,1)S(1)}, u32[]{:S(2)}, u32[]{:S(2)}) async-start(bf16[32,20,128]{2,1,0:T(8,128)(2,1)} %reshape.67), calls=%async_computation.1 | async-start | bytes 393216 | tf_op jit(solution)/shard_map/all_to_all | solution.py:145
Sparse Core Ops, SparseCore 0:
  224.2 82.3 all-gather.7
  312.7 32.6 all-gather.9
  348.3 32.1 all-gather.5
